TPU v7x, 512 devices: a whole 4x8x8 slice. The times are simulated.
512 devices in a mesh: section: 2 (over core), req: 64 (over y, z), head: 4 (over x).
Axes of the slice: x: 4, y: 8, z: 8, core: 2. Of those that a mesh axis runs over, the one named last changes fastest.
Arguments:
- embedding_per_slot: bfloat16 [512, 4, 1024], P('req', None, 'head'), may hold values from -6 to 6
- tally_per_slot: int32 [512], P('req'), may hold values from 1 to 4
- slot_requests: int32 [512], replicated, may hold values from 0 to 511, as said below
- memory_per_request: float32 [2, 512, 16, 64, 64], P('section', 'req', 'head'), may hold values from -4 to 4
- previous_step_feature: bfloat16 [2, 512, 1024], P('section', 'req', 'head'), may hold values from -6 to 6
- lag_interpolants: bfloat16 [2, 5, 1024], P('section'), may hold values from 0 to 1
- acceptor_projection: bfloat16 [2, 1024, 1024], P('section', None, 'head'), may hold values from -0.1875 to 0.1875
- address_projection: bfloat16 [2, 1024, 1024], P('section', None, 'head'), may hold values from -0.1875 to 0.1875
- content_projection: bfloat16 [2, 1024, 1024], P('section', None, 'head'), may hold values from -0.1875 to 0.1875
- readout_projection: bfloat16 [2, 1024, 1024], P('section', 'head'), may hold values from -0.1875 to 0.1875
- fading_first_lowrank: bfloat16 [2, 1024, 96], P('section', 'head'), may hold values from -0.1875 to 0.1875
- fading_second_lowrank: bfloat16 [2, 96, 1024], P('section', None, 'head'), may hold values from -0.625 to 0.625
- adapt_first_lowrank: bfloat16 [2, 1024, 96], P('section', 'head'), may hold values from -0.1875 to 0.1875
- adapt_second_lowrank: bfloat16 [2, 96, 1024], P('section', None, 'head'), may hold values from -0.625 to 0.625
- fading_baseline: float32 [2, 1024], P('section', 'head'), may hold values from -4 to 1
- adapt_baseline: float32 [2, 1024], P('section', 'head'), may hold values from -3 to 3
- erasing_address_gains: float32 [2, 1024], P('section', 'head'), may hold values from 0.5 to 1.5
- address_rate_coupling: float32 [2, 1024], P('section', 'head'), may hold values from 0 to 1
- present_extra_gain: float32 [2, 1024], P('section', 'head'), may hold values from -3 to 3
- section_standard_gains: float32 [2, 1024], P('section', 'head'), may hold values from 0.1 to 1.9
- section_standard_shift_terms: float32 [2, 1024], P('section', 'head'), may hold values from -2 to 2
Outputs:
- layer_out: bfloat16 [2, 512, 4, 1024], P('section', 'req', None, 'head')
Inputs may be any that keep to these rules, and one draw needn't show every extreme that they name: `slot_requests`: every request appears once. Of one group's 8 arrival slots at most 1 hold requests stored in any one group, and each group holds exactly 1 from some group.
All inputs are finite; a program needn't handle non-finite values.
Results may differ from a plain program's by a relative error of at most 0.02.
Values may be sent and summed in bfloat16 or wider, within the bound.
No kernel may reach another device: no remote copies, remote signals or barrier semaphores. Data moves between devices by JAX's collectives and lax.ppermute only.
A program may use at most 64 MiB of HBM per device.

v0:
```python
import jax
import jax.numpy as jnp
from jax import lax
from jax.sharding import PartitionSpec as P

highest = lax.Precision.HIGHEST


def from_behind(block, axis, distance):
    devices = range(lax.axis_size(axis))
    route = [(i - distance, i) for i in devices if i - distance in devices]
    return lax.ppermute(block, axis, route)


def sequence_recurrence(
    acceptor_entries,
    address_entries,
    content_entries,
    latent_response,
    adapt_latent,
    starting_memory,
    fading_second_lowrank,
    adapt_second_lowrank,
    fading_baseline,
    adapt_baseline,
    erasing_address_gains,
    address_rate_coupling,
    present_extra_gain,
    section_standard_gains,
    section_standard_shift_terms,
):
    batch_rows = starting_memory.shape[0]
    stored_memory_parts = starting_memory.shape[1]
    subspace_span = starting_memory.shape[2]

    def to_heads(array_in):
        return array_in.reshape(batch_rows, -1, stored_memory_parts, subspace_span)

    log_rate = (
        -jax.nn.softplus(
            -(
                fading_baseline
                + jnp.dot(
                    latent_response, fading_second_lowrank, preferred_element_type=jnp.float32
                )
            )
        )
        - 0.5
    )
    decays = to_heads(jnp.exp(-jnp.exp(log_rate)))
    learning = jax.nn.sigmoid(
        adapt_baseline
        + jnp.dot(adapt_latent, adapt_second_lowrank, preferred_element_type=jnp.float32)
    )
    learn_heads = to_heads(learning)
    scaled = to_heads(address_entries * erasing_address_gains)
    normed = scaled / jnp.sqrt(jnp.sum(scaled * scaled, axis=-1, keepdims=True) + 1e-06)
    erasing_address = to_heads(address_entries * (1.0 + (learning - 1.0) * address_rate_coupling))
    acceptor_parts = to_heads(acceptor_entries)
    content_part_lines = to_heads(content_entries)
    states = starting_memory
    readout = []
    for position in range(acceptor_parts.shape[1]):
        pulled = jnp.einsum("rhij,rhj->rhi", states, normed[:, position], precision=highest)
        states = (
            states * decays[:, position][:, :, None, :]
            - jnp.einsum(
                "rhi,rhj->rhij",
                pulled,
                normed[:, position] * learn_heads[:, position],
                precision=highest,
            )
            + jnp.einsum(
                "rhi,rhj->rhij",
                content_part_lines[:, position],
                erasing_address[:, position],
                precision=highest,
            )
        )
        readout.append(
            jnp.einsum("rhij,rhj->rhi", states, acceptor_parts[:, position], precision=highest)
        )
    read_all = jnp.stack(readout, axis=1)
    center = read_all - jnp.mean(read_all, axis=-1, keepdims=True)
    variance = jnp.mean(center * center, axis=-1, keepdims=True)
    gain_heads = section_standard_gains.reshape(stored_memory_parts, subspace_span)
    bias_heads = section_standard_shift_terms.reshape(stored_memory_parts, subspace_span)
    standardized_parts = center / jnp.sqrt(variance + 0.00064) * gain_heads + bias_heads
    present_extra_term = (
        jnp.sum(
            acceptor_parts
            * erasing_address
            * present_extra_gain.reshape(stored_memory_parts, subspace_span),
            axis=-1,
            keepdims=True,
        )
        * content_part_lines
    )
    return (
        (standardized_parts + present_extra_term)
        .astype(jnp.bfloat16)
        .reshape(-1, stored_memory_parts * subspace_span)
    )


def run_sublevel(lowrank_latent, earlier_entry, starting_memory, params):
    (
        lag_interpolants,
        acceptor_projection,
        address_projection,
        content_projection,
        readout_projection,
        fading_first_lowrank,
        fading_second_lowrank,
        adapt_first_lowrank,
        adapt_second_lowrank,
        fading_baseline,
        adapt_baseline,
        erasing_address_gains,
        address_rate_coupling,
        present_extra_gain,
        section_standard_gains,
        section_standard_shift_terms,
    ) = params
    batch_rows, steps_count, shard_width = lowrank_latent.shape
    previous = jnp.concatenate([earlier_entry[:, None, :], lowrank_latent[:, :-1, :]], axis=1)
    piece_now = lax.all_gather(lowrank_latent, "head", axis=2, tiled=True)
    piece_prev = lax.all_gather(previous, "head", axis=2, tiled=True)
    span_width = piece_now.shape[2]
    coef_rows = lag_interpolants.astype(jnp.float32)
    current_piece = piece_now.astype(jnp.float32)
    spread_piece = piece_prev.astype(jnp.float32) - current_piece
    updated = []
    for slot_num, which_mix, weight_all in (
        (0, 0, acceptor_projection),
        (1, 2, address_projection),
        (2, 3, content_projection),
    ):
        blend = (
            (current_piece + spread_piece * coef_rows[which_mix])
            .astype(jnp.bfloat16)
            .reshape(-1, span_width)
        )
        updated.append(jnp.dot(blend, weight_all, preferred_element_type=jnp.float32))
    acceptor_entries = updated[0]
    address_entries = updated[1]
    content_entries = updated[2]
    current = lowrank_latent.astype(jnp.float32)
    spread = previous.astype(jnp.float32) - current
    column_start = lax.axis_index("head") * shard_width
    decay_mix = lax.dynamic_slice_in_dim(lag_interpolants[1], column_start, shard_width, 0).astype(
        jnp.float32
    )
    learn_mix = lax.dynamic_slice_in_dim(lag_interpolants[4], column_start, shard_width, 0).astype(
        jnp.float32
    )
    decay_input = (current + spread * decay_mix).astype(jnp.bfloat16).reshape(-1, shard_width)
    learn_input = (current + spread * learn_mix).astype(jnp.bfloat16).reshape(-1, shard_width)
    partial_rank = jnp.dot(decay_input, fading_first_lowrank, preferred_element_type=jnp.float32)
    partial_learn = jnp.dot(learn_input, adapt_first_lowrank, preferred_element_type=jnp.float32)
    decay_total, learn_total = lax.psum((partial_rank, partial_learn), "head")
    latent_response = jnp.tanh(decay_total).astype(jnp.bfloat16)
    adapt_latent = learn_total.astype(jnp.bfloat16)
    lagged_features = sequence_recurrence(
        acceptor_entries,
        address_entries,
        content_entries,
        latent_response,
        adapt_latent,
        starting_memory,
        fading_second_lowrank,
        adapt_second_lowrank,
        fading_baseline,
        adapt_baseline,
        erasing_address_gains,
        address_rate_coupling,
        present_extra_gain,
        section_standard_gains,
        section_standard_shift_terms,
    )
    own_rows = lax.psum_scatter(
        lax.dot_general(
            readout_projection,
            lagged_features,
            (((0,), (1,)), ((), ())),
            preferred_element_type=jnp.float32,
        ),
        "head",
        scatter_dimension=0,
        tiled=True,
    )
    projected = own_rows.T.reshape(batch_rows, steps_count, shard_width)
    return (current + projected).astype(jnp.bfloat16)


def run_sections(inputs, states_use, last_use, params):
    section_num = lax.axis_index("section")
    section_count = lax.axis_size("section")
    block_count = 1
    block_rows = inputs.shape[0] // block_count
    result = jnp.zeros_like(inputs)
    incoming = jnp.zeros((block_rows,) + inputs.shape[1:], jnp.bfloat16)
    tick_total = block_count + section_count - 1
    for tick_num in range(tick_total):
        lag = tick_num - section_num
        entering = jnp.where(section_num == 0, inputs, incoming)
        produced = run_sublevel(entering, last_use, states_use, params)
        is_valid = (lag >= 0) & (lag < block_count)
        result = jnp.where(is_valid, produced, result)
        if tick_num + 1 < tick_total:
            incoming = from_behind(produced, "section", 1)
    return result


def body(
    embedding_per_slot,
    tally_per_slot,
    slot_requests,
    memory_per_request,
    previous_step_feature,
    lag_interpolants,
    acceptor_projection,
    address_projection,
    content_projection,
    readout_projection,
    fading_first_lowrank,
    fading_second_lowrank,
    adapt_first_lowrank,
    adapt_second_lowrank,
    fading_baseline,
    adapt_baseline,
    erasing_address_gains,
    address_rate_coupling,
    present_extra_gain,
    section_standard_gains,
    section_standard_shift_terms,
):
    local_rows = embedding_per_slot.shape[0]
    groups = lax.axis_size("req")
    capacity = (local_rows + groups - 1) // groups
    my_group = lax.axis_index("req")
    slot_ids = jnp.arange(local_rows, dtype=jnp.int32)
    table = slot_requests.reshape(groups, local_rows)
    my_arrivals = lax.dynamic_index_in_dim(table, my_group, 0, keepdims=False)
    home_group = my_arrivals // local_rows
    earlier = slot_ids[None, :] < slot_ids[:, None]
    arrival_rank = jnp.sum(
        ((home_group[:, None] == home_group[None, :]) & earlier).astype(jnp.int32), axis=1
    )
    arrival_slot = home_group * capacity + arrival_rank
    requests = my_group * local_rows + slot_ids
    total_rows = slot_requests.shape[0]
    found = slot_requests[None, :] == requests[:, None]
    positions = jnp.sum(
        jnp.where(found, jnp.arange(total_rows, dtype=jnp.int32)[None, :], 0), axis=1
    )
    source = positions // local_rows
    within = positions % local_rows
    source_homes = jnp.take(table, source, axis=0) // local_rows
    home_rank = jnp.sum(
        ((source_homes == my_group) & (slot_ids[None, :] < within[:, None])).astype(jnp.int32),
        axis=1,
    )
    home_slot = source * capacity + home_rank
    buffer_rows = groups * capacity
    params = (
        lag_interpolants[0],
        acceptor_projection[0],
        address_projection[0],
        content_projection[0],
        readout_projection[0],
        fading_first_lowrank[0],
        fading_second_lowrank[0],
        adapt_first_lowrank[0],
        adapt_second_lowrank[0],
        fading_baseline[0],
        adapt_baseline[0],
        erasing_address_gains[0],
        address_rate_coupling[0],
        present_extra_gain[0],
        section_standard_gains[0],
        section_standard_shift_terms[0],
    )
    states_local = memory_per_request[0]
    last_local = previous_step_feature[0]
    outgoing = (
        jnp.zeros((buffer_rows,) + embedding_per_slot.shape[1:], jnp.bfloat16)
        .at[arrival_slot]
        .set(embedding_per_slot)
    )
    arrived = lax.all_to_all(outgoing, "req", split_axis=0, concat_axis=0, tiled=True)
    inputs = jnp.take(arrived, home_slot, axis=0)
    result = run_sections(inputs, states_local, last_local, params)
    going_back = (
        jnp.zeros((buffer_rows,) + result.shape[1:], jnp.bfloat16).at[home_slot].set(result)
    )
    returned = lax.all_to_all(going_back, "req", split_axis=0, concat_axis=0, tiled=True)
    result = jnp.take(returned, arrival_slot, axis=0)
    live_mask = (
        jnp.arange(embedding_per_slot.shape[1], dtype=jnp.int32)[None, :] < tally_per_slot[:, None]
    )
    return jnp.where(live_mask[:, :, None], result, jnp.zeros_like(result))[None]


def solution(mesh):
    return jax.shard_map(
        body,
        mesh=mesh,
        in_specs=(
            P("req", None, "head"),
            P("req"),
            P(),
            P("section", "req", "head", None, None),
            P("section", "req", "head"),
            P("section", None, None),
            P("section", None, "head"),
            P("section", None, "head"),
            P("section", None, "head"),
            P("section", "head", None),
            P("section", "head", None),
            P("section", None, "head"),
            P("section", "head", None),
            P("section", None, "head"),
            P("section", "head"),
            P("section", "head"),
            P("section", "head"),
            P("section", "head"),
            P("section", "head"),
            P("section", "head"),
            P("section", "head"),
        ),
        out_specs=P("section", "req", None, "head"),
        check_vma=False,
    )
```

profile of v0, /device:TPU:8, one launch (start us, length us, event | category | flops | bytes accessed | tf_op | source)
XLA Modules:
  0.0 273.9 jit_solution(2103046319629629872)
XLA Ops:
  10.3 16.6 %all-to-all-start = ((bf16[64,4,256]{2,1,0:T(4,128)(2,1)}), bf16[64,4,256]{2,1,0:T(4,128)(2,1)S(1)}, u32[]{:S(2)}, u32[]{:S(2)}) async-start(bf16[64,4,256]{2,1,0:T(4,128)(2,1)} %scatter_fusion), calls=%async_computation | async-start | bytes 262144 | tf_op jit(solution)/shard_map/all_to_all | solution.py:291
  36.4 2.2 all-to-all-done
  39.2 12.3 %all_gather.12 = bf16[8,4,1024]{2,0,1:T(8,128)(2,1)S(1)} all-gather(bf16[8,4,256]{2,0,1:T(8,128)(2,1)S(1)} %broadcast_select_fusion.1), channel_id=1, replica_groups=mesh['section'=2,'req'=64,'head'=4] {'head'}, dimensions={2}, use_global_device_ids=true | all-gather | bytes 81920 | tf_op jit(solution)/shard_map/all_gather | solution.py:127
  51.5 11.9 %all_gather.13 = bf16[8,4,1024]{2,0,1:T(8,128)(2,1)S(1)} all-gather(bf16[8,4,256]{2,0,1:T(8,128)(2,1)S(1)} %pad_maximum_fusion.3), channel_id=1, replica_groups=mesh['section'=2,'req'=64,'head'=4] {'head'}, dimensions={2}, use_global_device_ids=true | all-gather | bytes 81920 | tf_op jit(solution)/shard_map/all_gather | solution.py:128
  65.4 16.7 %all-reduce.1 = (bf16[32,96]{1,0:T(8,128)(2,1)S(1)}, f32[32,96]{1,0:T(8,128)S(1)}) all-reduce(f32[32,96]{1,0:T(8,128)S(1)} %fusion.86, f32[32,96]{1,0:T(8,128)S(1)} %fusion.92), channel_id=1, replica_groups=mesh['section'=2,'req'=64,'head'=4] {'head'}, use_global_device_ids=true, to_apply=%region_6.8 | all-reduce | flops 6144 | bytes 43008 | tf_op jit(solution)/shard_map/psum | solution.py:161
  93.9 2.1 fusion.137
  96.7 2.1 fusion.160
  99.6 3.2 %fusion.55 = f32[8,4,1,64]{3,2,1,0:T(1,128)S(1)} fusion(f32[8,4,64]{2,1,0:T(4,128)S(1)} %copy-done.15, f32[8,4,64]{2,1,0:T(4,128)S(1)} %copy.164, f32[8,4,64]{2,1,0:T(4,128)S(1)} %copy-done.9, f32[8,4,64]{2,1,0:T(4,128)S(1)} %bitcast.461, f32[8,4,64]{2,1,0:T(4,128)S(1)} %get-tuple-element.50, f32[8,4,64,1]{2,0,1,3:T(8,128)S(1)} %copy-done.31, ...), kind=kOutput, calls=%fused_computation.72 | convolution fusion | flops 2883584 | bytes 622592 | tf_op jit(solution)/shard_map/rhij,rhj->rhi/dot_general | solution.py:81
  103.5 2.8 %fusion.54 = f32[8,4,1,64]{3,2,1,0:T(1,128)S(1)} fusion(f32[8,4,64,1]{2,3,1,0:T(1,128)S(1)} %bitcast.471, f32[8,4,64]{2,1,0:T(4,128)S(1)} %copy-done.15, f32[8,4,64]{2,1,0:T(4,128)S(1)} %copy.164, f32[8,4,64]{2,1,0:T(4,128)S(1)} %copy-done.9, f32[8,4,64]{2,1,0:T(4,128)S(1)} %bitcast.462, f32[8,4,64]{2,1,0:T(4,128)S(1)} %get-tuple-element.50, ...), kind=kOutput, calls=%fused_computation.71 | convolution fusion | flops 2883584 | bytes 622592 | tf_op jit(solution)/shard_map/rhij,rhj->rhi/dot_general | solution.py:64
  107.0 2.0 multiply_add_fusion.2
  114.0 2.1 fusion.32
  118.4 22.9 %reduce-scatter.3.cloned.1.call-done = f32[256,32]{0,1:T(8,128)} async-done(((f32[1024,32]{0,1:T(8,128)}), f32[256,32]{0,1:T(8,128)}) %reduce-scatter.3.cloned.1.call-update) | async-done | bytes 32784 | tf_op jit(solution)/shard_map/reduce_scatter | solution.py:181
  144.3 12.0 %all_gather.14 = bf16[8,4,1024]{2,0,1:T(8,128)(2,1)S(1)} all-gather(bf16[8,4,256]{2,0,1:T(8,128)(2,1)S(1)} %broadcast_select_fusion), channel_id=1, replica_groups=mesh['section'=2,'req'=64,'head'=4] {'head'}, dimensions={2}, use_global_device_ids=true | all-gather | bytes 81920 | tf_op jit(solution)/shard_map/all_gather | solution.py:127
  156.4 11.9 %all_gather.15 = bf16[8,4,1024]{2,0,1:T(8,128)(2,1)S(1)} all-gather(bf16[8,4,256]{2,0,1:T(8,128)(2,1)S(1)} %pad_maximum_fusion.2), channel_id=1, replica_groups=mesh['section'=2,'req'=64,'head'=4] {'head'}, dimensions={2}, use_global_device_ids=true | all-gather | bytes 81920 | tf_op jit(solution)/shard_map/all_gather | solution.py:128
  171.8 15.1 %all-reduce = (bf16[32,96]{1,0:T(8,128)(2,1)S(1)}, f32[32,96]{1,0:T(8,128)S(1)}) all-reduce(f32[32,96]{1,0:T(8,128)S(1)} %fusion.84, f32[32,96]{1,0:T(8,128)S(1)} %fusion.90), channel_id=1, replica_groups=mesh['section'=2,'req'=64,'head'=4] {'head'}, use_global_device_ids=true, to_apply=%region_13.15 | all-reduce | flops 6144 | bytes 43008 | tf_op jit(solution)/shard_map/psum | solution.py:161
  192.1 2.1 fusion.131
  194.1 2.1 fusion.155
  196.2 3.2 %fusion.57 = f32[8,4,1,64]{3,2,1,0:T(1,128)S(1)} fusion(f32[8,4,64]{2,1,0:T(4,128)S(1)} %get-tuple-element.42, f32[8,4,64]{2,1,0:T(4,128)S(1)} %copy.178, f32[8,4,64]{2,1,0:T(4,128)S(1)} %get-tuple-element.18, f32[8,4,64]{2,1,0:T(4,128)S(1)} %bitcast.464, f32[8,4,64]{2,1,0:T(4,128)S(1)} %get-tuple-element.30, f32[8,4,64,1]{2,0,1,3:T(8,128)S(1)} %get-tuple-element.27, ...), kind=kOutput, calls=%fused_computation.74 | convolution fusion | flops 2883584 | bytes 622592 | tf_op jit(solution)/shard_map/rhij,rhj->rhi/dot_general | solution.py:81
  199.5 2.8 %fusion.56 = f32[8,4,1,64]{3,2,1,0:T(1,128)S(1)} fusion(f32[8,4,64,1]{2,3,1,0:T(1,128)S(1)} %bitcast.473, f32[8,4,64]{2,1,0:T(4,128)S(1)} %get-tuple-element.42, f32[8,4,64]{2,1,0:T(4,128)S(1)} %copy.178, f32[8,4,64]{2,1,0:T(4,128)S(1)} %get-tuple-element.18, f32[8,4,64]{2,1,0:T(4,128)S(1)} %bitcast.465, f32[8,4,64]{2,1,0:T(4,128)S(1)} %get-tuple-element.30, ...), kind=kOutput, calls=%fused_computation.73 | convolution fusion | flops 2883584 | bytes 622592 | tf_op jit(solution)/shard_map/rhij,rhj->rhi/dot_general | solution.py:64
  202.3 2.0 multiply_add_fusion
  207.8 2.1 fusion.26
  213.6 23.6 %reduce-scatter.5.cloned.1.call-done = f32[256,32]{0,1:T(8,128)} async-done(((f32[1024,32]{0,1:T(8,128)}), f32[256,32]{0,1:T(8,128)}) %reduce-scatter.5.cloned.1.call-update) | async-done | bytes 32784 | tf_op jit(solution)/shard_map/reduce_scatter | solution.py:181
  240.6 13.4 %all-to-all-start.1 = ((bf16[64,4,256]{2,1,0:T(4,128)(2,1)}), bf16[64,4,256]{2,1,0:T(4,128)(2,1)S(1)}, u32[]{:S(2)}, u32[]{:S(2)}) async-start(bf16[64,4,256]{2,1,0:T(4,128)(2,1)} %scatter_fusion.1), calls=%async_computation.3 | async-start | bytes 262144 | tf_op jit(solution)/shard_map/all_to_all | solution.py:297
  254.7 11.1 %all-to-all-done.1 = bf16[64,4,256]{2,1,0:T(4,128)(2,1)S(1)} async-done(((bf16[64,4,256]{2,1,0:T(4,128)(2,1)}), bf16[64,4,256]{2,1,0:T(4,128)(2,1)S(1)}, u32[]{:S(2)}, u32[]{:S(2)}) %all-to-all-start.1) | async-done | bytes 131104 | tf_op jit(solution)/shard_map/all_to_all | solution.py:297
  (276 shorter events, 61.3 us)
Async XLA Ops:
  6.5 111.0 %copy-start = (bf16[1,256,1024]{2,1,0:T(8,128)(2,1)S(1)}, bf16[1,256,1024]{2,1,0:T(8,128)(2,1)}, u32[]{:S(2)}) copy-start(bf16[1,256,1024]{2,1,0:T(8,128)(2,1)} %param.32) | copy-start | bytes 1572868
  6.5 23.3 %copy-start.3 = (bf16[1,1024,256]{2,1,0:T(8,128)(2,1)S(1)}, bf16[1,1024,256]{2,1,0:T(8,128)(2,1)}, u32[]{:S(2)}) copy-start(bf16[1,1024,256]{2,1,0:T(8,128)(2,1)} %param.29) | copy-start | bytes 1572868
  7.4 20.9 %copy-start.8 = (s32[64,8]{1,0:T(8,128)}, s32[64,8]{1,0:T(8,128)S(1)}, u32[]{:S(2)}) copy-start(s32[64,8]{1,0:T(8,128)S(1)} %reshape.364) | copy-start | bytes 6148
  10.3 28.2 %all-to-all-start = ((bf16[64,4,256]{2,1,0:T(4,128)(2,1)}), bf16[64,4,256]{2,1,0:T(4,128)(2,1)S(1)}, u32[]{:S(2)}, u32[]{:S(2)}) async-start(bf16[64,4,256]{2,1,0:T(4,128)(2,1)} %scatter_fusion), calls=%async_computation | async-start | bytes 262144 | tf_op jit(solution)/shard_map/all_to_all | solution.py:291
  26.9 114.4 %reduce-scatter.3.cloned.1.call-start = ((), (), s32[]{:S(2)}) async-start(), calls=%async_computation.4 | async-start | bytes 163840 | tf_op jit(solution)/shard_map/reduce_scatter | solution.py:181
  29.7 33.8 %copy-start.33 = (pred[8]{0:T(512)(128)(4,1)}, pred[8]{0:T(512)(128)(4,1)S(1)}, u32[]{:S(2)}) copy-start(pred[8]{0:T(512)(128)(4,1)S(1)} %get-tuple-element.12) | copy-start | bytes 28
  29.8 33.8 %copy-start.35 = (f32[1,1,256]{2,1,0:T(1,128)}, f32[1,1,256]{2,1,0:T(1,128)S(1)}, u32[]{:S(2)}) copy-start(f32[1,1,256]{2,1,0:T(1,128)S(1)} %get-tuple-element.77) | copy-start | bytes 3076
  29.8 33.8 %copy-start.37 = (f32[1,1,256]{2,1,0:T(1,128)}, f32[1,1,256]{2,1,0:T(1,128)S(1)}, u32[]{:S(2)}) copy-start(f32[1,1,256]{2,1,0:T(1,128)S(1)} %get-tuple-element.78) | copy-start | bytes 3076
  36.4 27.0 %copy-start.23 = (f32[1,1,1024]{2,1,0:T(1,128)}, f32[1,1,1024]{2,1,0:T(1,128)S(1)}, u32[]{:S(2)}) copy-start(f32[1,1,1024]{2,1,0:T(1,128)S(1)} %get-tuple-element.73) | copy-start | bytes 12292
  36.4 49.2 %copy-start.21 = (f32[1,1,1024]{2,1,0:T(1,128)}, f32[1,1,1024]{2,1,0:T(1,128)S(1)}, u32[]{:S(2)}) copy-start(f32[1,1,1024]{2,1,0:T(1,128)S(1)} %get-tuple-element.72) | copy-start | bytes 12292
  39.2 12.3 %copy-start.17 = (bf16[1,8,256]{2,1,0:T(8,128)(2,1)S(1)}, bf16[1,8,256]{2,1,0:T(8,128)(2,1)}, u32[]{:S(2)}) copy-start(bf16[1,8,256]{2,1,0:T(8,128)(2,1)} %param.27) | copy-start | bytes 12292
  63.4 19.7 %copy-start.2 = (bf16[1,1024,256]{2,1,0:T(8,128)(2,1)S(1)}, bf16[1,1024,256]{2,1,0:T(8,128)(2,1)}, u32[]{:S(2)}) copy-start(bf16[1,1024,256]{2,1,0:T(8,128)(2,1)} %param.30) | copy-start | bytes 1572868
  65.2 16.9 %copy-start.55 = (bf16[1,96,256]{2,1,0:T(8,128)(2,1)S(1)}, bf16[1,96,256]{2,1,0:T(8,128)(2,1)}, u32[]{:S(2)}) copy-start(bf16[1,96,256]{2,1,0:T(8,128)(2,1)} %param.36) | copy-start | bytes 147460
  85.6 5.9 %copy-start.1 = (f32[1,8,4,64,64]{4,3,2,1,0:T(8,128)S(1)}, f32[1,8,4,64,64]{4,3,2,1,0:T(8,128)}, u32[]{:S(2)}) copy-start(f32[1,8,4,64,64]{4,3,2,1,0:T(8,128)} %param.26) | copy-start | bytes 1572868
  92.2 1.8 copy-start.32
  96.7 2.1 copy-start.31
  107.0 2.0 copy-start.12
  111.5 1.8 copy-start.28
  118.4 118.8 %reduce-scatter.5.cloned.1.call-start = ((), (), s32[]{:S(2)}) async-start(), calls=%async_computation.5 | async-start | bytes 163840 | tf_op jit(solution)/shard_map/reduce_scatter | solution.py:181
  142.1 2.1 collective-permute-start
  144.3 12.0 %copy-start.18 = (bf16[1,8,256]{2,1,0:T(8,128)(2,1)S(1)}, bf16[1,8,256]{2,1,0:T(8,128)(2,1)}, u32[]{:S(2)}) copy-start(bf16[1,8,256]{2,1,0:T(8,128)(2,1)} %param.27) | copy-start | bytes 12292
  156.4 11.9 %copy-start.22 = (f32[1,1,1024]{2,1,0:T(1,128)S(1)}, f32[1,1,1024]{2,1,0:T(1,128)}, u32[]{:S(2)}) copy-start(f32[1,1,1024]{2,1,0:T(1,128)} %copy-done.21) | copy-start | bytes 12292
  171.7 15.3 %copy-start.56 = (bf16[1,96,256]{2,1,0:T(8,128)(2,1)S(1)}, bf16[1,96,256]{2,1,0:T(8,128)(2,1)}, u32[]{:S(2)}) copy-start(bf16[1,96,256]{2,1,0:T(8,128)(2,1)} %param.36) | copy-start | bytes 147460
  240.6 25.1 %all-to-all-start.1 = ((bf16[64,4,256]{2,1,0:T(4,128)(2,1)}), bf16[64,4,256]{2,1,0:T(4,128)(2,1)S(1)}, u32[]{:S(2)}, u32[]{:S(2)}) async-start(bf16[64,4,256]{2,1,0:T(4,128)(2,1)} %scatter_fusion.1), calls=%async_computation.3 | async-start | bytes 262144 | tf_op jit(solution)/shard_map/all_to_all | solution.py:297
  (44 other events, 33.3 us)
Sparse Core Ops, SparseCore 0:
  118.5 22.7 reduce-scatter.2
  211.7 25.4 reduce-scatter.4
where the time goes:
time: 276 us; the launch traced here: 274 us
  blocking collectives  80 us (29%)
  waiting for transfers between devices  60.6 us (22%)
  matrix products  40.9 us (15%)
  local copies, waits for them, and re-layouts  35.8 us (13%)
  starting transfers between devices  31.3 us (11%)
  between operations  14.4 us (5%)
  other arithmetic  11 us (4%)
    reduce_scatter x2, waiting for transfers between devices, run_sublevel(): lax.psum_scatter(lax.dot_general(readout_projection, lagged_features, (((...  46.5 us
    psum x2, blocking collectives, run_sublevel(): decay_total, learn_total = lax.psum((partial_rank, partial_learn), 'head')  31.9 us
    all_gather x2, blocking collectives, run_sublevel(): piece_now = lax.all_gather(lowrank_latent, 'head', axis=2, tiled=True)  24.4 us
    all_gather x2, blocking collectives, run_sublevel(): piece_prev = lax.all_gather(previous, 'head', axis=2, tiled=True)  23.7 us
    unnamed x129, local copies, waits for them, and re-layouts  19.1 us
    dot_general x8, matrix products, sequence_recurrence(): jnp.einsum('rhij,rhj->rhi', states, acceptor_parts[:, position], precisio...  18.2 us
    dot_general x8, matrix products, sequence_recurrence(): jnp.einsum('rhij,rhj->rhi', states, normed[:, position], precision=highest)  16.7 us
    all_to_all x1, starting transfers between devices, body(): lax.all_to_all(outgoing, 'req', split_axis=0, concat_axis=0, tiled=True)  16.6 us
  transfers between devices with their start and end apart: 5, of which 5 were waited for; matrix products, arithmetic and copies ran while one was open for 3% of the time, Pallas kernels for 0%

commit v1 on v0

--- a/solution.py
+++ b/solution.py
@@ -125,7 +125,9 @@
     batch_rows, steps_count, shard_width = lowrank_latent.shape
     previous = jnp.concatenate([earlier_entry[:, None, :], lowrank_latent[:, :-1, :]], axis=1)
     piece_now = lax.all_gather(lowrank_latent, "head", axis=2, tiled=True)
-    piece_prev = lax.all_gather(previous, "head", axis=2, tiled=True)
+    piece_prev = jnp.concatenate(
+        lax.all_to_all(jnp.stack([previous] * lax.axis_size("head")), "head", 0, 0), axis=2
+    )
     span_width = piece_now.shape[2]
     coef_rows = lag_interpolants.astype(jnp.float32)
     current_piece = piece_now.astype(jnp.float32)

time: 276 us -> 266 us (0.964)
  blocking collectives: 80 us -> 58.9 us
  starting transfers between devices: 31.3 us -> 39.1 us
  local copies, waits for them, and re-layouts: 35.8 us -> 40.3 us
    all_gather x2 -> x0, blocking collectives: 23.7 us -> none  [run_sublevel(): piece_prev = lax.all_gather(previous, 'head', axis=2, tiled=True)]
    all_to_all x0 -> x2, starting transfers between devices: none -> 7.8 us  [run_sublevel(): lax.all_to_all(jnp.stack([previous] * lax.axis_size('head')), 'head', 0, 0)]
    unnamed x129 -> x131, local copies, waits for them, and re-layouts: 19.1 us -> 22.3 us
    psum x2, blocking collectives: 31.9 us -> 34.8 us  [run_sublevel(): decay_total, learn_total = lax.psum((partial_rank, partial_learn), 'head')]
  transfers between devices with their start and end apart: 5 -> 7, of which waited for: 5 -> 5; matrix products, arithmetic and copies ran while one was open for 3% -> 4% of each run, Pallas kernels for 0% -> 0%
where the time goes in v1:
time: 266 us; the launch traced here: 264 us
  waiting for transfers between devices  60.6 us (23%)
  blocking collectives  58.9 us (22%)
  local copies, waits for them, and re-layouts  40.3 us (15%)
  matrix products  40 us (15%)
  starting transfers between devices  39.1 us (15%)
  between operations  14.4 us (5%)
  other arithmetic  10.9 us (4%)
    reduce_scatter x2, waiting for transfers between devices, run_sublevel(): lax.psum_scatter(lax.dot_general(readout_projection, lagged_features, (((...  46.5 us
    psum x2, blocking collectives, run_sublevel(): decay_total, learn_total = lax.psum((partial_rank, partial_learn), 'head')  34.8 us
    all_gather x2, blocking collectives, run_sublevel(): piece_now = lax.all_gather(lowrank_latent, 'head', axis=2, tiled=True)  24.1 us
    unnamed x131, local copies, waits for them, and re-layouts  22.3 us
    dot_general x8, matrix products, sequence_recurrence(): jnp.einsum('rhij,rhj->rhi', states, acceptor_parts[:, position], precisio...  18.2 us
    dot_general x8, matrix products, sequence_recurrence(): jnp.einsum('rhij,rhj->rhi', states, normed[:, position], precision=highest)  16.7 us
    all_to_all x1, starting transfers between devices, body(): lax.all_to_all(outgoing, 'req', split_axis=0, concat_axis=0, tiled=True)  16.6 us
    all_to_all x1, starting transfers between devices, body(): lax.all_to_all(going_back, 'req', split_axis=0, concat_axis=0, tiled=True)  13.4 us
  transfers between devices with their start and end apart: 7, of which 5 were waited for; matrix products, arithmetic and copies ran while one was open for 4% of the time, Pallas kernels for 0%

profile of v1, /device:TPU:8, one launch (start us, length us, event | category | flops | bytes accessed | tf_op | source)
XLA Modules:
  0.0 264.3 jit_solution(10844532490726261195)
XLA Ops:
  10.9 16.6 %all-to-all-start = ((bf16[64,4,256]{2,1,0:T(4,128)(2,1)}), bf16[64,4,256]{2,1,0:T(4,128)(2,1)S(1)}, u32[]{:S(2)}, u32[]{:S(2)}) async-start(bf16[64,4,256]{2,1,0:T(4,128)(2,1)} %scatter_fusion), calls=%async_computation | async-start | bytes 262144 | tf_op jit(solution)/shard_map/all_to_all | solution.py:293
  36.9 2.2 all-to-all-done
  41.0 4.3 %all-to-all-start.1 = ((bf16[4,8,4,256]{3,2,1,0:T(4,128)(2,1)}), bf16[4,8,4,256]{3,2,1,0:T(4,128)(2,1)S(1)}, u32[]{:S(2)}, u32[]{:S(2)}) async-start(bf16[4,8,4,256]{3,2,1,0:T(4,128)(2,1)} %stack.44), calls=%async_computation.1 | async-start | bytes 131072 | tf_op jit(solution)/shard_map/all_to_all | solution.py:129
  47.1 17.6 %all-reduce.1 = (bf16[32,96]{1,0:T(8,128)(2,1)S(1)}, f32[32,96]{1,0:T(8,128)S(1)}) all-reduce(f32[32,96]{1,0:T(8,128)S(1)} %fusion.86, f32[32,96]{1,0:T(8,128)S(1)} %fusion.92), channel_id=1, replica_groups=mesh['section'=2,'req'=64,'head'=4] {'head'}, use_global_device_ids=true, to_apply=%region_6.8 | all-reduce | flops 6144 | bytes 43008 | tf_op jit(solution)/shard_map/psum | solution.py:163
  67.3 12.2 %all_gather.6 = bf16[8,4,1024]{2,0,1:T(8,128)(2,1)S(1)} all-gather(bf16[8,4,256]{2,0,1:T(8,128)(2,1)S(1)} %broadcast_select_fusion.1), channel_id=1, replica_groups=mesh['section'=2,'req'=64,'head'=4] {'head'}, dimensions={2}, use_global_device_ids=true | all-gather | bytes 81920 | tf_op jit(solution)/shard_map/all_gather | solution.py:127
  88.8 2.1 fusion.137
  91.6 2.1 fusion.160
  94.4 3.2 %fusion.55 = f32[8,4,1,64]{3,2,1,0:T(1,128)S(1)} fusion(f32[8,4,64]{2,1,0:T(4,128)S(1)} %get-tuple-element.62, f32[8,4,64]{2,1,0:T(4,128)S(1)} %copy.174, f32[8,4,64]{2,1,0:T(4,128)S(1)} %copy-done.9, f32[8,4,64]{2,1,0:T(4,128)S(1)} %bitcast.473, f32[8,4,64]{2,1,0:T(4,128)S(1)} %copy-done.12, f32[8,4,64,1]{2,0,1,3:T(8,128)S(1)} %copy-done.31, ...), kind=kOutput, calls=%fused_computation.72 | convolution fusion | flops 2883584 | bytes 622592 | tf_op jit(solution)/shard_map/rhij,rhj->rhi/dot_general | solution.py:81
  98.4 2.8 %fusion.54 = f32[8,4,1,64]{3,2,1,0:T(1,128)S(1)} fusion(f32[8,4,64,1]{2,3,1,0:T(1,128)S(1)} %bitcast.483, f32[8,4,64]{2,1,0:T(4,128)S(1)} %get-tuple-element.62, f32[8,4,64]{2,1,0:T(4,128)S(1)} %copy.174, f32[8,4,64]{2,1,0:T(4,128)S(1)} %copy-done.9, f32[8,4,64]{2,1,0:T(4,128)S(1)} %bitcast.474, f32[8,4,64]{2,1,0:T(4,128)S(1)} %copy-done.12, ...), kind=kOutput, calls=%fused_computation.71 | convolution fusion | flops 2883584 | bytes 622592 | tf_op jit(solution)/shard_map/rhij,rhj->rhi/dot_general | solution.py:64
  101.9 2.0 multiply_add_fusion.2
  108.9 2.1 fusion.32
  113.3 22.8 %reduce-scatter.3.cloned.1.call-done = f32[256,32]{0,1:T(8,128)} async-done(((f32[1024,32]{0,1:T(8,128)}), f32[256,32]{0,1:T(8,128)}) %reduce-scatter.3.cloned.1.call-update) | async-done | bytes 32784 | tf_op jit(solution)/shard_map/reduce_scatter | solution.py:183
  141.1 3.5 %all-to-all-start.2 = ((bf16[4,8,4,256]{3,2,1,0:T(4,128)(2,1)}), bf16[4,8,4,256]{3,2,1,0:T(4,128)(2,1)S(1)}, u32[]{:S(2)}, u32[]{:S(2)}) async-start(bf16[4,8,4,256]{3,2,1,0:T(4,128)(2,1)} %stack.50), calls=%async_computation.3 | async-start | bytes 131072 | tf_op jit(solution)/shard_map/all_to_all | solution.py:129
  145.8 17.3 %all-reduce = (bf16[32,96]{1,0:T(8,128)(2,1)S(1)}, f32[32,96]{1,0:T(8,128)S(1)}) all-reduce(f32[32,96]{1,0:T(8,128)S(1)} %fusion.84, f32[32,96]{1,0:T(8,128)S(1)} %fusion.90), channel_id=1, replica_groups=mesh['section'=2,'req'=64,'head'=4] {'head'}, use_global_device_ids=true, to_apply=%region_13.15 | all-reduce | flops 6144 | bytes 43008 | tf_op jit(solution)/shard_map/psum | solution.py:163
  165.0 11.9 %all_gather.7 = bf16[8,4,1024]{2,0,1:T(8,128)(2,1)S(1)} all-gather(bf16[8,4,256]{2,0,1:T(8,128)(2,1)S(1)} %broadcast_select_fusion), channel_id=1, replica_groups=mesh['section'=2,'req'=64,'head'=4] {'head'}, dimensions={2}, use_global_device_ids=true | all-gather | bytes 81920 | tf_op jit(solution)/shard_map/all_gather | solution.py:127
  182.5 2.1 fusion.131
  184.6 2.1 fusion.155
  186.7 3.2 %fusion.57 = f32[8,4,1,64]{3,2,1,0:T(1,128)S(1)} fusion(f32[8,4,64]{2,1,0:T(4,128)S(1)} %get-tuple-element.42, f32[8,4,64]{2,1,0:T(4,128)S(1)} %copy.190, f32[8,4,64]{2,1,0:T(4,128)S(1)} %get-tuple-element.18, f32[8,4,64]{2,1,0:T(4,128)S(1)} %bitcast.476, f32[8,4,64]{2,1,0:T(4,128)S(1)} %get-tuple-element.30, f32[8,4,64,1]{2,0,1,3:T(8,128)S(1)} %get-tuple-element.27, ...), kind=kOutput, calls=%fused_computation.74 | convolution fusion | flops 2883584 | bytes 622592 | tf_op jit(solution)/shard_map/rhij,rhj->rhi/dot_general | solution.py:81
  189.9 2.8 %fusion.56 = f32[8,4,1,64]{3,2,1,0:T(1,128)S(1)} fusion(f32[8,4,64,1]{2,3,1,0:T(1,128)S(1)} %bitcast.485, f32[8,4,64]{2,1,0:T(4,128)S(1)} %get-tuple-element.42, f32[8,4,64]{2,1,0:T(4,128)S(1)} %copy.190, f32[8,4,64]{2,1,0:T(4,128)S(1)} %get-tuple-element.18, f32[8,4,64]{2,1,0:T(4,128)S(1)} %bitcast.477, f32[8,4,64]{2,1,0:T(4,128)S(1)} %get-tuple-element.30, ...), kind=kOutput, calls=%fused_computation.73 | convolution fusion | flops 2883584 | bytes 622592 | tf_op jit(solution)/shard_map/rhij,rhj->rhi/dot_general | solution.py:64
  192.8 2.0 multiply_add_fusion
  198.3 2.1 fusion.26
  204.0 23.7 %reduce-scatter.5.cloned.1.call-done = f32[256,32]{0,1:T(8,128)} async-done(((f32[1024,32]{0,1:T(8,128)}), f32[256,32]{0,1:T(8,128)}) %reduce-scatter.5.cloned.1.call-update) | async-done | bytes 32784 | tf_op jit(solution)/shard_map/reduce_scatter | solution.py:183
  231.1 13.4 %all-to-all-start.3 = ((bf16[64,4,256]{2,1,0:T(4,128)(2,1)}), bf16[64,4,256]{2,1,0:T(4,128)(2,1)S(1)}, u32[]{:S(2)}, u32[]{:S(2)}) async-start(bf16[64,4,256]{2,1,0:T(4,128)(2,1)} %scatter_fusion.1), calls=%async_computation.5 | async-start | bytes 262144 | tf_op jit(solution)/shard_map/all_to_all | solution.py:299
  245.1 11.1 %all-to-all-done.3 = bf16[64,4,256]{2,1,0:T(4,128)(2,1)S(1)} async-done(((bf16[64,4,256]{2,1,0:T(4,128)(2,1)}), bf16[64,4,256]{2,1,0:T(4,128)(2,1)S(1)}, u32[]{:S(2)}, u32[]{:S(2)}) %all-to-all-start.3) | async-done | bytes 131104 | tf_op jit(solution)/shard_map/all_to_all | solution.py:299
  (288 shorter events, 64.9 us)
Async XLA Ops:
  6.5 105.8 %copy-start = (bf16[1,256,1024]{2,1,0:T(8,128)(2,1)S(1)}, bf16[1,256,1024]{2,1,0:T(8,128)(2,1)}, u32[]{:S(2)}) copy-start(bf16[1,256,1024]{2,1,0:T(8,128)(2,1)} %param.32) | copy-start | bytes 1572868
  6.5 23.8 %copy-start.3 = (bf16[1,1024,256]{2,1,0:T(8,128)(2,1)S(1)}, bf16[1,1024,256]{2,1,0:T(8,128)(2,1)}, u32[]{:S(2)}) copy-start(bf16[1,1024,256]{2,1,0:T(8,128)(2,1)} %param.29) | copy-start | bytes 1572868
  7.4 21.5 %copy-start.8 = (s32[64,8]{1,0:T(8,128)}, s32[64,8]{1,0:T(8,128)S(1)}, u32[]{:S(2)}) copy-start(s32[64,8]{1,0:T(8,128)S(1)} %reshape.376) | copy-start | bytes 6148
  10.9 28.2 %all-to-all-start = ((bf16[64,4,256]{2,1,0:T(4,128)(2,1)}), bf16[64,4,256]{2,1,0:T(4,128)(2,1)S(1)}, u32[]{:S(2)}, u32[]{:S(2)}) async-start(bf16[64,4,256]{2,1,0:T(4,128)(2,1)} %scatter_fusion), calls=%async_computation | async-start | bytes 262144 | tf_op jit(solution)/shard_map/all_to_all | solution.py:293
  30.2 15.1 %copy-start.33 = (pred[8]{0:T(512)(128)(4,1)}, pred[8]{0:T(512)(128)(4,1)S(1)}, u32[]{:S(2)}) copy-start(pred[8]{0:T(512)(128)(4,1)S(1)} %get-tuple-element.12) | copy-start | bytes 28
  30.3 15.0 %copy-start.35 = (f32[1,1,256]{2,1,0:T(1,128)}, f32[1,1,256]{2,1,0:T(1,128)S(1)}, u32[]{:S(2)}) copy-start(f32[1,1,256]{2,1,0:T(1,128)S(1)} %get-tuple-element.77) | copy-start | bytes 3076
  30.3 15.0 %copy-start.37 = (f32[1,1,256]{2,1,0:T(1,128)}, f32[1,1,256]{2,1,0:T(1,128)S(1)}, u32[]{:S(2)}) copy-start(f32[1,1,256]{2,1,0:T(1,128)S(1)} %get-tuple-element.78) | copy-start | bytes 3076
  36.9 42.6 %copy-start.21 = (f32[1,1,1024]{2,1,0:T(1,128)}, f32[1,1,1024]{2,1,0:T(1,128)S(1)}, u32[]{:S(2)}) copy-start(f32[1,1,1024]{2,1,0:T(1,128)S(1)} %get-tuple-element.73) | copy-start | bytes 12292
  41.0 38.5 %all-to-all-start.1 = ((bf16[4,8,4,256]{3,2,1,0:T(4,128)(2,1)}), bf16[4,8,4,256]{3,2,1,0:T(4,128)(2,1)S(1)}, u32[]{:S(2)}, u32[]{:S(2)}) async-start(bf16[4,8,4,256]{3,2,1,0:T(4,128)(2,1)} %stack.44), calls=%async_computation.1 | async-start | bytes 131072 | tf_op jit(solution)/shard_map/all_to_all | solution.py:129
  45.3 90.8 %reduce-scatter.3.cloned.1.call-start = ((), (), s32[]{:S(2)}) async-start(), calls=%async_computation.6 | async-start | bytes 163840 | tf_op jit(solution)/shard_map/reduce_scatter | solution.py:183
  47.0 17.7 %copy-start.57 = (bf16[1,96,256]{2,1,0:T(8,128)(2,1)S(1)}, bf16[1,96,256]{2,1,0:T(8,128)(2,1)}, u32[]{:S(2)}) copy-start(bf16[1,96,256]{2,1,0:T(8,128)(2,1)} %param.34) | copy-start | bytes 147460
  67.3 12.4 %copy-start.2 = (bf16[1,1024,256]{2,1,0:T(8,128)(2,1)S(1)}, bf16[1,1024,256]{2,1,0:T(8,128)(2,1)}, u32[]{:S(2)}) copy-start(bf16[1,1024,256]{2,1,0:T(8,128)(2,1)} %param.30) | copy-start | bytes 1572868
  83.4 2.9 %copy-start.1 = (f32[1,8,4,64,64]{4,3,2,1,0:T(8,128)S(1)}, f32[1,8,4,64,64]{4,3,2,1,0:T(8,128)}, u32[]{:S(2)}) copy-start(f32[1,8,4,64,64]{4,3,2,1,0:T(8,128)} %param.26) | copy-start | bytes 1572868
  87.0 1.7 copy-start.10
  87.0 1.7 copy-start.13
  87.0 1.8 copy-start.32
  91.6 2.1 copy-start.31
  101.9 2.0 copy-start.15
  106.4 1.8 copy-start.28
  136.9 2.1 collective-permute-start
  141.1 35.7 %all-to-all-start.2 = ((bf16[4,8,4,256]{3,2,1,0:T(4,128)(2,1)}), bf16[4,8,4,256]{3,2,1,0:T(4,128)(2,1)S(1)}, u32[]{:S(2)}, u32[]{:S(2)}) async-start(bf16[4,8,4,256]{3,2,1,0:T(4,128)(2,1)} %stack.50), calls=%async_computation.3 | async-start | bytes 131072 | tf_op jit(solution)/shard_map/all_to_all | solution.py:129
  144.7 83.0 %reduce-scatter.5.cloned.1.call-start = ((), (), s32[]{:S(2)}) async-start(), calls=%async_computation.7 | async-start | bytes 163840 | tf_op jit(solution)/shard_map/reduce_scatter | solution.py:183
  145.7 17.4 %copy-start.56 = (bf16[1,96,256]{2,1,0:T(8,128)(2,1)S(1)}, bf16[1,96,256]{2,1,0:T(8,128)(2,1)}, u32[]{:S(2)}) copy-start(bf16[1,96,256]{2,1,0:T(8,128)(2,1)} %param.36) | copy-start | bytes 147460
  231.1 25.1 %all-to-all-start.3 = ((bf16[64,4,256]{2,1,0:T(4,128)(2,1)}), bf16[64,4,256]{2,1,0:T(4,128)(2,1)S(1)}, u32[]{:S(2)}, u32[]{:S(2)}) async-start(bf16[64,4,256]{2,1,0:T(4,128)(2,1)} %scatter_fusion.1), calls=%async_computation.5 | async-start | bytes 262144 | tf_op jit(solution)/shard_map/all_to_all | solution.py:299
  (47 other events, 33.1 us)
Sparse Core Ops, SparseCore 0:
  113.4 22.6 reduce-scatter.2
  202.1 25.4 reduce-scatter.4
